TPU v7x, 256 devices: a whole 4x4x8 slice. The times are simulated.
256 devices in a mesh: dp: 8 (over x, core), seq: 32 (over y, z).
Axes of the slice: x: 4, y: 4, z: 8, core: 2. Of those that a mesh axis runs over, the one named last changes fastest.
Arguments:
- activations: bfloat16 [8, 4096, 2048], P('dp', 'seq'), may hold values from -16 to 16
- w_query: bfloat16 [2048, 2048], P('seq')
- w_key: bfloat16 [2048, 256], P('seq')
- w_value: bfloat16 [2048, 256], P('seq'), may hold values from -0.125 to 0.125
- key_blocks: int32 [32, 32, 7], replicated, may hold values from 0 to 31, as said below
- random_count: int32 [32], replicated, may hold values from 1 to 3, 64 in all
- grad_out: bfloat16 [8, 4096, 2048], P('dp', 'seq'), may hold values from -6 to 6
Outputs:
- attn_out: bfloat16 [8, 4096, 2048], P('dp', 'seq')
- grad_x: bfloat16 [8, 4096, 2048], P('dp', 'seq')
- grad_wq: bfloat16 [2048, 2048], P('seq')
- grad_wk: bfloat16 [2048, 256], P('seq')
- grad_wv: bfloat16 [2048, 256], P('seq')
Inputs may be any that keep to these rules, and one draw needn't show every extreme that they name: `key_blocks`: row b of head h: columns 0 to 2 are b - 1, b and b + 1 modulo 32; column 3 is one block of the head, the same in all its rows; columns 4 to 6 are three blocks that differ from each other and from the row's first four entries. Head h uses the first random_count[h] of its three random key blocks; the counts sum to 64.
All inputs are finite; a program needn't handle non-finite values.
Results may differ from a plain program's by a relative error of at most 0.025.
The roundings to bfloat16 on the way count: a program that leaves them out, or rounds other values in their place, can miss the bound.
Values may be sent and summed in bfloat16 or wider, within the bound.
No kernel may reach another device: no remote copies, remote signals or barrier semaphores. Data moves between devices by JAX's collectives and lax.ppermute only.
A program may use at most 128 MiB of HBM per device.

v0:
```python
import math
import jax
import jax.numpy as jnp
from jax import lax
from jax.sharding import PartitionSpec as P

HD = 64
GROUP = 8
masked_score = -1e30
query_group = 4
RING_Z = 8


def head_pass(queries, key_rows, value_rows, grad_head, blocks, extra_count):
    seq_len, head_width = queries.shape
    block_count, slot_count = blocks.shape
    block_len = seq_len // block_count
    score_scale = head_width ** (-0.5)
    key_tiles = key_rows.reshape(block_count, block_len, head_width)
    value_tiles = value_rows.reshape(block_count, block_len, head_width)
    q_part = queries.reshape(block_count, block_len, head_width)
    g_part = grad_head.reshape(block_count, block_len, head_width)
    usable = jnp.repeat(jnp.arange(slot_count) < 4 + extra_count, block_len)
    k_part = key_tiles[blocks].reshape(block_count, slot_count * block_len, head_width)
    v_part = value_tiles[blocks].reshape(block_count, slot_count * block_len, head_width)
    scores = (
        jnp.einsum("gqe,gke->gqk", q_part, k_part, preferred_element_type=jnp.float32) * score_scale
    )
    scores = jnp.where(usable, scores, masked_score)
    highest = jnp.max(scores, axis=-1, keepdims=True)
    exponent = jnp.exp(scores - highest)
    shares = exponent / jnp.sum(exponent, axis=-1, keepdims=True)
    shares_low = shares.astype(jnp.bfloat16)
    attended = jnp.einsum(
        "gqk,gke->gqe", shares_low, v_part, preferred_element_type=jnp.float32
    ).astype(jnp.bfloat16)
    grad_shares = jnp.einsum("gqe,gke->gqk", g_part, v_part, preferred_element_type=jnp.float32)
    weighted = jnp.sum(grad_shares * shares, axis=-1, keepdims=True)
    grad_scores = (shares * (grad_shares - weighted)).astype(jnp.bfloat16)
    grad_query = (
        jnp.einsum("gqk,gke->gqe", grad_scores, k_part, preferred_element_type=jnp.float32)
        * score_scale
    ).astype(jnp.bfloat16)
    grad_keys = (
        jnp.einsum("gqk,gqe->gke", grad_scores, q_part, preferred_element_type=jnp.float32)
        * score_scale
    )
    grad_values = jnp.einsum("gqk,gqe->gke", shares_low, g_part, preferred_element_type=jnp.float32)
    pieces = jnp.concatenate([grad_keys, grad_values], axis=-1).reshape(
        block_count * slot_count, block_len * 2 * head_width
    )
    owner = (
        blocks.reshape(1, block_count * slot_count)
        == jnp.arange(block_count, dtype=blocks.dtype)[:, None]
    ).astype(jnp.float32)
    summed = jnp.dot(owner, pieces, precision=lax.Precision.HIGHEST)
    return (
        attended.reshape(seq_len, head_width),
        grad_query.reshape(seq_len, head_width),
        summed.reshape(seq_len, 2 * head_width),
    )


def ring_reduce_scatter(parts, ring, stride, position):
    seq_devices = lax.axis_size("seq")
    group = ring * stride
    me = position // stride % ring
    width = parts.shape[-1] // 2
    ahead = [
        (s, s // group * group + (s // stride % ring + 1) % ring * stride + s % stride)
        for s in range(seq_devices)
    ]
    behind = [(b, a) for a, b in ahead]
    total = []
    for side, perm, sign in ((0, ahead, 1), (1, behind, -1)):
        own = parts[..., side * width : (side + 1) * width]

        def chunk(k):
            return lax.dynamic_index_in_dim(own, (me - sign * (1 + k)) % ring, 0, keepdims=False)

        buf = chunk(0)
        for k in range(ring - 1):
            got = lax.ppermute(buf, "seq", perm)
            buf = (got.astype(jnp.float32) + chunk(k + 1).astype(jnp.float32)).astype(jnp.bfloat16)
        total.append(buf)
    return jnp.concatenate(total, axis=-1)


def per_device(activations, w_query, w_key, w_value, key_blocks, random_count, grad_out):
    seq_devices = lax.axis_size("seq")
    dp_devices = lax.axis_size("dp")
    position = lax.axis_index("seq")
    dp_index = lax.axis_index("dp")
    tokens = activations[0]
    grad_rows = grad_out[0]
    tok_count = tokens.shape[0]
    heads = w_query.shape[1] // HD
    kv_heads = w_key.shape[1] // HD
    query_cols = heads * HD
    kv_cols = kv_heads * HD
    all_cols = query_cols + 2 * kv_cols
    w_local = jnp.concatenate([w_query, w_key, w_value], axis=1)
    w_full = lax.all_gather(w_local, "seq", axis=0, tiled=True)
    projected = jnp.dot(tokens, w_full, preferred_element_type=jnp.float32).astype(jnp.bfloat16)
    queries = projected[:, :query_cols]
    key_proj = projected[:, query_cols : query_cols + kv_cols]
    value_proj = projected[:, query_cols + kv_cols :]
    query_pieces = queries.reshape(tok_count, heads, HD).transpose(1, 0, 2)
    grad_pieces = grad_rows.reshape(tok_count, heads, HD).transpose(1, 0, 2)
    paired = jnp.concatenate(
        [key_proj.reshape(tok_count, kv_heads, HD), value_proj.reshape(tok_count, kv_heads, HD)],
        axis=2,
    )
    kv_pieces = jnp.repeat(paired.transpose(1, 0, 2), GROUP, axis=0)
    sent = jnp.concatenate([query_pieces, grad_pieces, kv_pieces], axis=2)
    landed = lax.all_to_all(sent, "seq", split_axis=0, concat_axis=1, tiled=True)[0]
    head_q = landed[:, :HD]
    head_grad = landed[:, HD : 2 * HD]
    head_k = landed[:, 2 * HD : 3 * HD]
    head_v = landed[:, 3 * HD :]
    blocks_mine = lax.dynamic_index_in_dim(key_blocks, position, 0, keepdims=False)
    count_mine = lax.dynamic_index_in_dim(random_count, position, 0, keepdims=False)
    attended, grad_query, grad_kv = head_pass(
        head_q, head_k, head_v, head_grad, blocks_mine, count_mine
    )
    back_sent = jnp.concatenate(
        [
            attended.reshape(seq_devices, tok_count, HD),
            grad_query.reshape(seq_devices, tok_count, HD),
            grad_kv.astype(jnp.bfloat16).reshape(seq_devices, tok_count, 2 * HD),
        ],
        axis=2,
    )
    back = lax.all_to_all(back_sent, "seq", split_axis=0, concat_axis=0, tiled=True)
    back_out = back[:, :, :HD]
    back_query = back[:, :, HD : 2 * HD]
    back_kv = back[:, :, 2 * HD :]
    out_rows = back_out.transpose(1, 0, 2).reshape(tok_count, heads * HD)
    grad_q_rows = back_query.transpose(1, 0, 2).reshape(tok_count, heads * HD)
    kv_sum = jnp.sum(
        back_kv.reshape(kv_heads, GROUP, tok_count, 2 * HD), axis=1, dtype=jnp.float32
    ).astype(jnp.bfloat16)
    grad_k_rows = kv_sum[:, :, :HD].transpose(1, 0, 2).reshape(tok_count, kv_heads * HD)
    grad_v_rows = kv_sum[:, :, HD:].transpose(1, 0, 2).reshape(tok_count, kv_heads * HD)
    combined = jnp.concatenate([grad_q_rows, grad_k_rows, grad_v_rows], axis=1)
    contract = (((1,), (1,)), ((), ()))
    grad_x_rows = lax.dot_general(
        combined, w_full, contract, preferred_element_type=jnp.float32
    ).astype(jnp.bfloat16)
    factor = 1.0 / math.sqrt(tok_count * seq_devices * dp_devices)
    over_tokens = (((0,), (0,)), ((), ()))
    term = (
        lax.dot_general(tokens, combined, over_tokens, preferred_element_type=jnp.float32) * factor
    ).astype(jnp.bfloat16)
    half = all_cols // 2
    core = dp_index % 2
    pairs = [(i, i ^ 1) for i in range(dp_devices)]
    keep = lax.dynamic_slice_in_dim(term, core * half, half, axis=1)
    give = lax.dynamic_slice_in_dim(term, (1 - core) * half, half, axis=1)
    got = lax.ppermute(give, "dp", pairs)
    chip_sum = (keep.astype(jnp.float32) + got.astype(jnp.float32)).astype(jnp.bfloat16)
    rows = chip_sum.shape[0] // seq_devices
    by_z = chip_sum.reshape(seq_devices // RING_Z, RING_Z, rows, half).transpose(1, 0, 2, 3)
    by_y = ring_reduce_scatter(by_z, RING_Z, 1, position)
    part = ring_reduce_scatter(by_y, seq_devices // RING_Z, RING_Z, position)
    step = 2
    while step < dp_devices:
        mates = [(i, i ^ step) for i in range(dp_devices)]
        other = lax.ppermute(part, "dp", mates)
        part = (part.astype(jnp.float32) + other.astype(jnp.float32)).astype(jnp.bfloat16)
        step *= 2
    other_half = lax.ppermute(part, "dp", pairs)
    first = jnp.where(core == 0, part, other_half)
    second = jnp.where(core == 0, other_half, part)
    grad_all = jnp.concatenate([first, second], axis=1)
    grad_wq = grad_all[:, :query_cols]
    grad_wk = grad_all[:, query_cols : query_cols + kv_cols]
    grad_wv = grad_all[:, query_cols + kv_cols :]
    return (out_rows[None], grad_x_rows[None], grad_wq, grad_wk, grad_wv)


def solution(mesh):
    placed = (
        P("dp", "seq", None),
        P("seq", None),
        P("seq", None),
        P("seq", None),
        P(),
        P(),
        P("dp", "seq", None),
    )
    return jax.shard_map(
        per_device,
        mesh=mesh,
        in_specs=placed,
        out_specs=(
            P("dp", "seq", None),
            P("dp", "seq", None),
            P("seq", None),
            P("seq", None),
            P("seq", None),
        ),
        check_vma=False,
    )
```

profile of v0, /device:TPU:1, one launch (start us, length us, event | category | flops | bytes accessed | tf_op | source)
XLA Modules:
  0.0 566.1 jit_solution(12210671963242412984)
XLA Ops:
  10.4 113.4 %all-gather.2.cloned.1.call-done = bf16[2048,2560]{1,0:T(8,128)(2,1)} async-done(((bf16[64,2560]{1,0:T(8,128)(2,1)}), bf16[2048,2560]{1,0:T(8,128)(2,1)}) %all-gather.2.cloned.1.call-update) | async-done | bytes 10485776 | tf_op jit(solution)/shard_map/all_gather | solution.py:103
  123.7 6.9 %fusion.13 = bf16[128,2560]{0,1:T(8,128)(2,1)S(1)} fusion(bf16[2048,2560]{1,0:T(8,128)(2,1)} %all-gather.2.cloned.1.call-done, bf16[1,128,2048]{2,1,0:T(8,128)(2,1)S(1)} %copy-done), kind=kOutput, calls=%fused_computation.27 | convolution fusion | flops 1342504960 | bytes 11665408 | tf_op jit(solution)/shard_map/dot_general | solution.py:104
  132.5 5.6 all-to-all-start
  140.7 46.1 %all-to-all-done = bf16[32,128,256]{1,2,0:T(8,128)(2,1)} async-done(((bf16[32,128,256]{1,2,0:T(8,128)(2,1)}), bf16[32,128,256]{1,2,0:T(8,128)(2,1)}, u32[]{:S(2)}, u32[]{:S(2)}) %all-to-all-start) | async-done | bytes 2097184 | tf_op jit(solution)/shard_map/all_to_all | solution.py:116
  186.7 3.3 copy.117
  190.0 2.7 fusion.73
  195.9 2.9 gather_fusion
  198.8 6.2 %copy.122 = bf16[224,128,64]{1,0,2:T(8,128)(2,1)} copy(bf16[224,128,64]{1,2,0:T(8,128)(2,1)} %gather_fusion) | data formatting | bytes 7340032 | tf_op jit(solution)/shard_map/gather | solution.py:24
  205.0 7.8 %reshape.152 = bf16[32,896,64]{1,0,2:T(8,128)(2,1)} reshape(bf16[224,128,64]{1,0,2:T(8,128)(2,1)} %copy.122) | data formatting | bytes 7340032 | tf_op jit(solution)/shard_map/reshape | solution.py:24
  212.8 3.0 gather_fusion.1
  215.8 6.2 %copy.127 = bf16[224,128,64]{1,0,2:T(8,128)(2,1)} copy(bf16[224,128,64]{1,2,0:T(8,128)(2,1)} %gather_fusion.1) | data formatting | bytes 7340032 | tf_op jit(solution)/shard_map/gather | solution.py:25
  222.0 7.8 %reshape.154 = bf16[32,896,64]{1,0,2:T(8,128)(2,1)} reshape(bf16[224,128,64]{1,0,2:T(8,128)(2,1)} %copy.127) | data formatting | bytes 7340032 | tf_op jit(solution)/shard_map/reshape | solution.py:25
  229.8 10.8 %fusion.77 = (f32[32,128]{1,0:T(8,128)S(1)}, f32[32,128,896]{2,1,0:T(8,128)}) fusion(pred[896]{0:T(1024)(128)(4,1)S(1)} %broadcast_bitcast_fusion, bf16[32,128,64]{2,1,0:T(8,128)(2,1)S(1)} %bitcast.152, bf16[32,896,64]{1,0,2:T(8,128)(2,1)} %reshape.152), kind=kOutput, calls=%fused_computation.119 | convolution fusion | flops 484443008 | bytes 18891648 | tf_op jit(solution)/shard_map/sub | solution.py:31
  240.6 9.3 %fusion.31 = bf16[32,128,64]{1,2,0:T(8,128)(2,1)S(1)} fusion(bf16[32,896,64]{1,0,2:T(8,128)(2,1)} %reshape.154, f32[32,128,896]{2,1,0:T(8,128)} %get-tuple-element.49, f32[32,128]{1,0:T(8,128)S(1)} %get-tuple-element.48), kind=kOutput, calls=%fused_computation.42 | convolution fusion | flops 477364224 | bytes 18890752 | tf_op jit(solution)/shard_map/gqk,gke->gqe/dot_general | solution.py:34
  249.9 9.8 %fusion.9 = f32[32,896,64]{1,2,0:T(8,128)} fusion(bf16[32,128,64]{2,1,0:T(8,128)(2,1)S(1)} %bitcast.162, f32[32,128,896]{2,1,0:T(8,128)} %get-tuple-element.49, f32[32,128]{1,0:T(8,128)S(1)} %get-tuple-element.48), kind=kOutput, calls=%fused_computation.22 | convolution fusion | flops 477102080 | bytes 22560768 | tf_op jit(solution)/shard_map/gqk,gqe->gke/dot_general | solution.py:48
  259.7 11.0 %multiply_reduce_fusion = (f32[32,128]{1,0:T(8,128)S(1)}, f32[32,128,896]{2,1,0:T(8,128)}) fusion(f32[32,128,896]{2,1,0:T(8,128)} %get-tuple-element.49, f32[32,128]{1,0:T(8,128)S(1)} %get-tuple-element.48, bf16[32,128,64]{2,1,0:T(8,128)(2,1)S(1)} %bitcast.163, bf16[32,896,64]{1,0,2:T(8,128)(2,1)S(1)} %copy-done.7), kind=kOutput, calls=%fused_computation.9 | convolution fusion | flops 480768000 | bytes 33587200 | tf_op jit(solution)/shard_map/gqe,gke->gqk/dot_general | solution.py:37
  270.7 10.8 %multiply_convert_fusion.1 = bf16[32,128,896]{2,1,0:T(8,128)(2,1)S(1)} fusion(f32[32,128,896]{2,1,0:T(8,128)} %get-tuple-element.51, f32[32,128]{1,0:T(8,128)S(1)} %get-tuple-element.50, f32[32,128,896]{2,1,0:T(8,128)} %get-tuple-element.49, f32[32,128]{1,0:T(8,128)S(1)} %get-tuple-element.48), kind=kLoop, calls=%fused_computation.8 | loop fusion | flops 14680064 | bytes 36732928 | tf_op jit(solution)/shard_map/convert_element_type | solution.py:39
  281.5 3.4 fusion.28
  284.8 4.3 broadcast_multiply_fusion
  290.8 10.5 %pad_maximum_fusion = f32[32,896,128]{1,2,0:T(8,128)} fusion(f32[32,896,64]{1,2,0:T(8,128)} %fusion.9, f32[32,896,64]{1,2,0:T(8,128)} %broadcast_multiply_fusion), kind=kLoop, calls=%fused_computation.7 | loop fusion | flops 3670016 | bytes 29360128 | tf_op jit(solution)/shard_map/concatenate | solution.py:49
  301.3 16.1 %copy.136 = f32[32,896,128]{2,1,0:T(8,128)} copy(f32[32,896,128]{1,2,0:T(8,128)} %pad_maximum_fusion) | data formatting | bytes 29360128 | tf_op jit(solution)/shard_map/concatenate | solution.py:49
  317.4 16.0 %reshape.156 = f32[224,16384]{1,0:T(8,128)} reshape(f32[32,896,128]{2,1,0:T(8,128)} %copy.136) | data formatting | bytes 29360128 | tf_op jit(solution)/shard_map/reshape | solution.py:49
  335.1 9.1 %fusion.22 = bf16[32,128,128]{2,0,1:T(8,128)(2,1)S(1)} fusion(s32[224]{0:T(256)S(1)} %eq.47, f32[224,16384]{1,0:T(8,128)} %reshape.156), kind=kOutput, calls=%fused_computation.39 | convolution fusion | flops 1409817600 | bytes 15729536 | tf_op jit(solution)/shard_map/dot_general | solution.py:56
  345.3 2.5 copy.140
  347.9 7.1 %all-to-all-start.1 = ((bf16[32,128,256]{2,1,0:T(8,128)(2,1)}), bf16[32,128,256]{2,1,0:T(8,128)(2,1)S(1)}, u32[]{:S(2)}, u32[]{:S(2)}) async-start(bf16[32,128,256]{2,1,0:T(8,128)(2,1)} %copy.140), calls=%async_computation.1 | async-start | bytes 4194304 | tf_op jit(solution)/shard_map/all_to_all | solution.py:134
  355.0 48.6 %all-to-all-done.1 = bf16[32,128,256]{2,1,0:T(8,128)(2,1)S(1)} async-done(((bf16[32,128,256]{2,1,0:T(8,128)(2,1)}), bf16[32,128,256]{2,1,0:T(8,128)(2,1)S(1)}, u32[]{:S(2)}, u32[]{:S(2)}) %all-to-all-start.1) | async-done | bytes 2097184 | tf_op jit(solution)/shard_map/all_to_all | solution.py:134
  407.9 4.2 multiply_convert_fusion
  412.2 2.9 dynamic-slice_bitcast_fusion
  415.1 2.7 copy-done.1
  420.3 8.6 %collective-permute-done = bf16[2048,1280]{1,0:T(8,128)(2,1)} collective-permute-done((bf16[2048,1280]{1,0:T(8,128)(2,1)}, bf16[2048,1280]{1,0:T(8,128)(2,1)}, u32[]{:S(2)}, u32[]{:S(2)}) %collective-permute-start) | collective-permute-done | bytes 5242912 | tf_op jit(solution)/shard_map/ppermute | solution.py:160
  428.9 5.4 fusion.5
  439.9 7.0 %collective-permute-done.11 = bf16[4,64,640]{2,1,0:T(8,128)(2,1)} collective-permute-done((bf16[4,64,640]{2,1,0:T(8,128)(2,1)}, bf16[4,64,640]{2,1,0:T(8,128)(2,1)}, u32[]{:S(2)}, u32[]{:S(2)}) %collective-permute-start.11) | collective-permute-done | bytes 327712 | tf_op jit(solution)/shard_map/ppermute | solution.py:83
  452.5 4.8 collective-permute-done.12
  459.2 2.9 collective-permute-start.13
  463.9 3.4 collective-permute-done.13
  469.2 3.4 collective-permute-start.14
  474.4 2.5 collective-permute-done.14
  478.8 3.1 collective-permute-start.15
  488.1 3.1 collective-permute-start.16
  497.4 3.1 collective-permute-start.17
  501.7 3.2 collective-permute-done.17
  515.2 3.0 collective-permute-start.20
  519.8 4.4 collective-permute-done.10
  525.5 3.3 collective-permute-done.21
  528.8 2.8 collective-permute-start.22
  531.6 3.0 collective-permute-done.22
  534.7 13.0 %collective-permute-start.23 = (bf16[64,1280]{1,0:T(8,128)(2,1)S(1)}, bf16[64,1280]{1,0:T(8,128)(2,1)S(1)}, u32[]{:S(2)}, u32[]{:S(2)}) collective-permute-start(bf16[64,1280]{1,0:T(8,128)(2,1)S(1)} %add_convert_fusion), channel_id=1, source_target_pairs={{0,32},{32,0},{64,96},{96,64},{128,160},{160,128},{192,224},{224,1... | collective-permute-start | bytes 491528 | tf_op jit(solution)/shard_map/ppermute | solution.py:172
  547.7 8.5 %fusion.21 = bf16[1,128,2048]{2,1,0:T(8,128)(2,1)} fusion(bf16[2048,2560]{1,0:T(8,128)(2,1)} %all-gather.2.cloned.1.call-done, bf16[128,256]{0,1:T(8,128)(2,1)S(1)} %bitcast.165, bf16[128,256]{0,1:T(8,128)(2,1)S(1)} %bitcast.167, bf16[128,2048]{0,1:T(8,128)(2,1)} %bitcast.155), kind=kOutput, calls=%fused_computation.36 | convolution fusion | flops 1344405504 | bytes 11665408 | tf_op jit(solution)/shard_map/dot_general | solution.py:147
  (116 shorter events, 70.9 us)
Async XLA Ops:
  7.2 116.6 %copy-start = (bf16[1,128,2048]{2,1,0:T(8,128)(2,1)S(1)}, bf16[1,128,2048]{2,1,0:T(8,128)(2,1)}, u32[]{:S(2)}) copy-start(bf16[1,128,2048]{2,1,0:T(8,128)(2,1)} %param.7) | copy-start | bytes 1572868
  7.2 116.6 %all-gather.2.cloned.1.call-start = ((), (), s32[]{:S(2)}) async-start(), calls=%async_computation.2 | async-start | bytes 10813440 | tf_op jit(solution)/shard_map/all_gather | solution.py:103
  130.7 7.5 %copy-start.10 = (s32[32]{0:T(128)S(1)}, s32[32]{0:T(128)}, u32[]{:S(2)}) copy-start(s32[32]{0:T(128)} %param.12) | copy-start | bytes 388
  132.5 54.2 %all-to-all-start = ((bf16[32,128,256]{1,2,0:T(8,128)(2,1)}), bf16[32,128,256]{1,2,0:T(8,128)(2,1)}, u32[]{:S(2)}, u32[]{:S(2)}) async-start(bf16[32,128,256]{1,2,0:T(8,128)(2,1)} %pad_maximum_fusion.1), calls=%async_computation | async-start | bytes 4194304 | tf_op jit(solution)/shard_map/all_to_all | solution.py:116
  222.0 7.8 %copy-start.3 = (bf16[4096,64]{1,0:T(8,128)(2,1)S(1)}, bf16[4096,64]{1,0:T(8,128)(2,1)}, u32[]{:S(2)}) copy-start(bf16[4096,64]{1,0:T(8,128)(2,1)} %get-tuple-element.39) | copy-start | bytes 1572868
  240.6 9.3 %copy-start.8 = (bf16[4096,64]{1,0:T(8,128)(2,1)S(1)}, bf16[4096,64]{1,0:T(8,128)(2,1)}, u32[]{:S(2)}) copy-start(bf16[4096,64]{1,0:T(8,128)(2,1)} %get-tuple-element.37) | copy-start | bytes 1572868
  249.9 9.8 %copy-start.7 = (bf16[32,896,64]{1,0,2:T(8,128)(2,1)S(1)}, bf16[32,896,64]{1,0,2:T(8,128)(2,1)}, u32[]{:S(2)}) copy-start(bf16[32,896,64]{1,0,2:T(8,128)(2,1)} %reshape.154) | copy-start | bytes 11010052
  270.7 10.8 %copy-start.6 = (bf16[32,896,64]{1,0,2:T(8,128)(2,1)S(1)}, bf16[32,896,64]{1,0,2:T(8,128)(2,1)}, u32[]{:S(2)}) copy-start(bf16[32,896,64]{1,0,2:T(8,128)(2,1)} %reshape.152) | copy-start | bytes 11010052
  317.4 16.1 %copy-start.9 = (bf16[32,128,64]{1,2,0:T(8,128)(2,1)S(1)}, bf16[32,128,64]{1,2,0:T(8,128)(2,1)}, u32[]{:S(2)}) copy-start(bf16[32,128,64]{1,2,0:T(8,128)(2,1)} %fusion.28) | copy-start | bytes 1572868
  347.9 55.8 %all-to-all-start.1 = ((bf16[32,128,256]{2,1,0:T(8,128)(2,1)}), bf16[32,128,256]{2,1,0:T(8,128)(2,1)S(1)}, u32[]{:S(2)}, u32[]{:S(2)}) async-start(bf16[32,128,256]{2,1,0:T(8,128)(2,1)} %copy.140), calls=%async_computation.1 | async-start | bytes 4194304 | tf_op jit(solution)/shard_map/all_to_all | solution.py:134
  407.2 5.0 copy-start.4
  412.1 5.7 %copy-start.1 = (bf16[2560,2048]{0,1:T(8,128)(2,1)}, bf16[2560,2048]{0,1:T(8,128)(2,1)S(1)}, u32[]{:S(2)}) copy-start(bf16[2560,2048]{0,1:T(8,128)(2,1)S(1)} %multiply_convert_fusion) | copy-start | bytes 31457284
  417.8 11.1 %collective-permute-start = (bf16[2048,1280]{1,0:T(8,128)(2,1)}, bf16[2048,1280]{1,0:T(8,128)(2,1)}, u32[]{:S(2)}, u32[]{:S(2)}) collective-permute-start(bf16[2048,1280]{1,0:T(8,128)(2,1)} %dynamic-slice_bitcast_fusion), channel_id=1, source_target_pairs={{0,32},{32,0},{64,96},{96,64},{128,160},{160,128},{192,224},{224,1... | collective-permute-start | bytes 15728648 | tf_op jit(solution)/shard_map/ppermute | solution.py:160
  435.4 1.5 copy-start.2
  437.7 9.2 %collective-permute-start.11 = (bf16[4,64,640]{2,1,0:T(8,128)(2,1)}, bf16[4,64,640]{2,1,0:T(8,128)(2,1)}, u32[]{:S(2)}, u32[]{:S(2)}) collective-permute-start(bf16[4,64,640]{2,1,0:T(8,128)(2,1)} %dynamic-slice_bitcast_fusion.1), channel_id=1, source_target_pairs={{1,0},{2,1},{3,2},{4,3},{5,4},{6,5},{7,6},{0,7},{9,8},{10,9},{11,1... | collective-permute-start | bytes 983048 | tf_op jit(solution)/shard_map/ppermute | solution.py:83
  438.9 11.7 %collective-permute-start.1 = (bf16[4,64,640]{2,1,0:T(8,128)(2,1)}, bf16[4,64,640]{2,1,0:T(8,128)(2,1)}, u32[]{:S(2)}, u32[]{:S(2)}) collective-permute-start(bf16[4,64,640]{2,1,0:T(8,128)(2,1)} %dynamic-slice_bitcast_fusion.2), channel_id=1, source_target_pairs={{0,1},{1,2},{2,3},{3,4},{4,5},{5,6},{6,7},{7,0},{8,9},{9,10},{10,1... | collective-permute-start | bytes 983048 | tf_op jit(solution)/shard_map/ppermute | solution.py:83
  448.8 8.5 %collective-permute-start.12 = (bf16[4,64,640]{2,1,0:T(8,128)(2,1)}, bf16[4,64,640]{2,1,0:T(8,128)(2,1)}, u32[]{:S(2)}, u32[]{:S(2)}) collective-permute-start(bf16[4,64,640]{2,1,0:T(8,128)(2,1)} %fusion.46), channel_id=1, source_target_pairs={{1,0},{2,1},{3,2},{4,3},{5,4},{6,5},{7,6},{0,7},{9,8},{10,9},{11,1... | collective-permute-start | bytes 983048 | tf_op jit(solution)/shard_map/ppermute | solution.py:83
  452.5 9.6 %collective-permute-start.2 = (bf16[4,64,640]{2,1,0:T(8,128)(2,1)}, bf16[4,64,640]{2,1,0:T(8,128)(2,1)}, u32[]{:S(2)}, u32[]{:S(2)}) collective-permute-start(bf16[4,64,640]{2,1,0:T(8,128)(2,1)} %fusion.53), channel_id=1, source_target_pairs={{0,1},{1,2},{2,3},{3,4},{4,5},{5,6},{6,7},{7,0},{8,9},{9,10},{10,1... | collective-permute-start | bytes 983048 | tf_op jit(solution)/shard_map/ppermute | solution.py:83
  459.2 8.1 %collective-permute-start.13 = (bf16[4,64,640]{2,1,0:T(8,128)(2,1)}, bf16[4,64,640]{2,1,0:T(8,128)(2,1)}, u32[]{:S(2)}, u32[]{:S(2)}) collective-permute-start(bf16[4,64,640]{2,1,0:T(8,128)(2,1)} %fusion.45), channel_id=1, source_target_pairs={{1,0},{2,1},{3,2},{4,3},{5,4},{6,5},{7,6},{0,7},{9,8},{10,9},{11,1... | collective-permute-start | bytes 983048 | tf_op jit(solution)/shard_map/ppermute | solution.py:83
  463.9 8.7 %collective-permute-start.3 = (bf16[4,64,640]{2,1,0:T(8,128)(2,1)}, bf16[4,64,640]{2,1,0:T(8,128)(2,1)}, u32[]{:S(2)}, u32[]{:S(2)}) collective-permute-start(bf16[4,64,640]{2,1,0:T(8,128)(2,1)} %fusion.52), channel_id=1, source_target_pairs={{0,1},{1,2},{2,3},{3,4},{4,5},{5,6},{6,7},{7,0},{8,9},{9,10},{10,1... | collective-permute-start | bytes 983048 | tf_op jit(solution)/shard_map/ppermute | solution.py:83
  469.2 7.7 %collective-permute-start.14 = (bf16[4,64,640]{2,1,0:T(8,128)(2,1)}, bf16[4,64,640]{2,1,0:T(8,128)(2,1)}, u32[]{:S(2)}, u32[]{:S(2)}) collective-permute-start(bf16[4,64,640]{2,1,0:T(8,128)(2,1)} %fusion.44), channel_id=1, source_target_pairs={{1,0},{2,1},{3,2},{4,3},{5,4},{6,5},{7,6},{0,7},{9,8},{10,9},{11,1... | collective-permute-start | bytes 983048 | tf_op jit(solution)/shard_map/ppermute | solution.py:83
  474.4 7.5 %collective-permute-start.4 = (bf16[4,64,640]{2,1,0:T(8,128)(2,1)}, bf16[4,64,640]{2,1,0:T(8,128)(2,1)}, u32[]{:S(2)}, u32[]{:S(2)}) collective-permute-start(bf16[4,64,640]{2,1,0:T(8,128)(2,1)} %fusion.51), channel_id=1, source_target_pairs={{0,1},{1,2},{2,3},{3,4},{4,5},{5,6},{6,7},{7,0},{8,9},{9,10},{10,1... | collective-permute-start | bytes 983048 | tf_op jit(solution)/shard_map/ppermute | solution.py:83
  478.8 7.5 %collective-permute-start.15 = (bf16[4,64,640]{2,1,0:T(8,128)(2,1)}, bf16[4,64,640]{2,1,0:T(8,128)(2,1)}, u32[]{:S(2)}, u32[]{:S(2)}) collective-permute-start(bf16[4,64,640]{2,1,0:T(8,128)(2,1)} %fusion.43), channel_id=1, source_target_pairs={{1,0},{2,1},{3,2},{4,3},{5,4},{6,5},{7,6},{0,7},{9,8},{10,9},{11,1... | collective-permute-start | bytes 983048 | tf_op jit(solution)/shard_map/ppermute | solution.py:83
  483.7 7.5 %collective-permute-start.5 = (bf16[4,64,640]{2,1,0:T(8,128)(2,1)}, bf16[4,64,640]{2,1,0:T(8,128)(2,1)}, u32[]{:S(2)}, u32[]{:S(2)}) collective-permute-start(bf16[4,64,640]{2,1,0:T(8,128)(2,1)} %fusion.50), channel_id=1, source_target_pairs={{0,1},{1,2},{2,3},{3,4},{4,5},{5,6},{6,7},{7,0},{8,9},{9,10},{10,1... | collective-permute-start | bytes 983048 | tf_op jit(solution)/shard_map/ppermute | solution.py:83
  488.1 7.5 %collective-permute-start.16 = (bf16[4,64,640]{2,1,0:T(8,128)(2,1)}, bf16[4,64,640]{2,1,0:T(8,128)(2,1)}, u32[]{:S(2)}, u32[]{:S(2)}) collective-permute-start(bf16[4,64,640]{2,1,0:T(8,128)(2,1)} %fusion.42), channel_id=1, source_target_pairs={{1,0},{2,1},{3,2},{4,3},{5,4},{6,5},{7,6},{0,7},{9,8},{10,9},{11,1... | collective-permute-start | bytes 983048 | tf_op jit(solution)/shard_map/ppermute | solution.py:83
  493.0 7.5 %collective-permute-start.6 = (bf16[4,64,640]{2,1,0:T(8,128)(2,1)}, bf16[4,64,640]{2,1,0:T(8,128)(2,1)}, u32[]{:S(2)}, u32[]{:S(2)}) collective-permute-start(bf16[4,64,640]{2,1,0:T(8,128)(2,1)} %fusion.49), channel_id=1, source_target_pairs={{0,1},{1,2},{2,3},{3,4},{4,5},{5,6},{6,7},{7,0},{8,9},{9,10},{10,1... | collective-permute-start | bytes 983048 | tf_op jit(solution)/shard_map/ppermute | solution.py:83
  497.4 7.5 %collective-permute-start.17 = (bf16[4,64,640]{2,1,0:T(8,128)(2,1)}, bf16[4,64,640]{2,1,0:T(8,128)(2,1)}, u32[]{:S(2)}, u32[]{:S(2)}) collective-permute-start(bf16[4,64,640]{2,1,0:T(8,128)(2,1)} %fusion.41), channel_id=1, source_target_pairs={{1,0},{2,1},{3,2},{4,3},{5,4},{6,5},{7,6},{0,7},{9,8},{10,9},{11,1... | collective-permute-start | bytes 983048 | tf_op jit(solution)/shard_map/ppermute | solution.py:83
  501.6 8.4 %collective-permute-start.7 = (bf16[4,64,640]{2,1,0:T(8,128)(2,1)S(1)}, bf16[4,64,640]{2,1,0:T(8,128)(2,1)S(1)}, u32[]{:S(2)}, u32[]{:S(2)}) collective-permute-start(bf16[4,64,640]{2,1,0:T(8,128)(2,1)S(1)} %fusion.48), channel_id=1, source_target_pairs={{0,1},{1,2},{2,3},{3,4},{4,5},{5,6},{6,7},{7,0},{8,9},{9,10},{10,1... | collective-permute-start | bytes 983048 | tf_op jit(solution)/shard_map/ppermute | solution.py:83
  506.1 5.2 collective-permute-start.18
  510.1 4.9 collective-permute-start.8
  511.3 3.9 collective-permute-start.19
  515.0 4.6 collective-permute-start.9
  515.2 4.5 collective-permute-start.20
  519.6 4.6 collective-permute-start.10
  524.2 4.6 collective-permute-start.21
  528.8 5.8 %collective-permute-start.22 = (bf16[64,1280]{1,0:T(8,128)(2,1)S(1)}, bf16[64,1280]{1,0:T(8,128)(2,1)S(1)}, u32[]{:S(2)}, u32[]{:S(2)}) collective-permute-start(bf16[64,1280]{1,0:T(8,128)(2,1)S(1)} %add_convert_fusion.1), channel_id=1, source_target_pairs={{0,128},{32,160},{64,192},{96,224},{128,0},{160,32},{192,64},{224,... | collective-permute-start | bytes 491528 | tf_op jit(solution)/shard_map/ppermute | solution.py:169
  534.7 21.6 %copy-start.5 = (bf16[32,128,64]{2,1,0:T(8,128)(2,1)S(1)}, bf16[32,128,64]{2,1,0:T(8,128)(2,1)}, u32[]{:S(2)}) copy-start(bf16[32,128,64]{2,1,0:T(8,128)(2,1)} %get-tuple-element.35) | copy-start | bytes 1572868
  534.7 22.9 %collective-permute-start.23 = (bf16[64,1280]{1,0:T(8,128)(2,1)S(1)}, bf16[64,1280]{1,0:T(8,128)(2,1)S(1)}, u32[]{:S(2)}, u32[]{:S(2)}) collective-permute-start(bf16[64,1280]{1,0:T(8,128)(2,1)S(1)} %add_convert_fusion), channel_id=1, source_target_pairs={{0,32},{32,0},{64,96},{96,64},{128,160},{160,128},{192,224},{224,1... | collective-permute-start | bytes 491528 | tf_op jit(solution)/shard_map/ppermute | solution.py:172
Sparse Core Ops, SparseCore 0:
  11.2 112.5 all-gather.1
where the time goes:
time: 572 us; the launch traced here: 566 us
  waiting for transfers between devices  258 us (45%)
  local copies, waits for them, and re-layouts  99.6 us (17%)
  matrix products  77.2 us (13%)
  starting transfers between devices  60.2 us (11%)
  other arithmetic  55.6 us (10%)
  between operations  15.4 us (3%)
    all_gather x1, waiting for transfers between devices, per_device(): w_full = lax.all_gather(w_local, 'seq', axis=0, tiled=True)  113 us
    all_to_all x1, waiting for transfers between devices, per_device(): lax.all_to_all(back_sent, 'seq', split_axis=0, concat_axis=0, tiled=True)  48.6 us
    all_to_all x1, waiting for transfers between devices, per_device(): lax.all_to_all(sent, 'seq', split_axis=0, concat_axis=1, tiled=True)[0]  46.1 us
    ppermute x20, waiting for transfers between devices, ring_reduce_scatter(): got = lax.ppermute(buf, 'seq', perm)  35.1 us
    ppermute x20, starting transfers between devices, ring_reduce_scatter(): got = lax.ppermute(buf, 'seq', perm)  27.9 us
    convert_element_type x20, other arithmetic, ring_reduce_scatter(): (got.astype(jnp.float32) + chunk(k + 1).astype(jnp.float32)).astype(jnp.b...  22.7 us
    concatenate x1, local copies, waits for them, and re-layouts, head_pass(): jnp.concatenate([grad_keys, grad_values], axis=-1)  16.1 us
    reshape x1, local copies, waits for them, and re-layouts, head_pass(): jnp.concatenate([grad_keys, grad_values], axis=-1)  16 us
  transfers between devices with their start and end apart: 27, of which 18 were waited for; matrix products, arithmetic and copies ran while one was open for 6% of the time, Pallas kernels for 0%

commit v1 on v0

--- a/solution.py
+++ b/solution.py
@@ -100,7 +100,15 @@
     kv_cols = kv_heads * HD
     all_cols = query_cols + 2 * kv_cols
     w_local = jnp.concatenate([w_query, w_key, w_value], axis=1)
-    w_full = lax.all_gather(w_local, "seq", axis=0, tiled=True)
+    w_full = jnp.concatenate(
+        lax.all_to_all(
+            jnp.stack([w_local for _ in range(lax.axis_size("seq"))]),
+            axis_name="seq",
+            split_axis=0,
+            concat_axis=0,
+        ),
+        axis=0,
+    )
     projected = jnp.dot(tokens, w_full, preferred_element_type=jnp.float32).astype(jnp.bfloat16)
     queries = projected[:, :query_cols]
     key_proj = projected[:, query_cols : query_cols + kv_cols]

time: 572 us -> 707 us (1.24)
  waiting for transfers between devices: 258 us -> 383 us
  starting transfers between devices: 60.2 us -> 80 us
  between operations: 15.4 us -> 2.23 us
    all_to_all x0 -> x1, waiting for transfers between devices: none -> 238 us  [per_device(): lax.all_to_all(jnp.stack([w_local for _ in range(lax.axis_size('seq'))]),...]
    all_gather x1 -> x0, waiting for transfers between devices: 113 us -> none  [per_device(): w_full = lax.all_gather(w_local, 'seq', axis=0, tiled=True)]
    all_to_all x0 -> x1, starting transfers between devices: none -> 12.3 us  [per_device(): lax.all_to_all(jnp.stack([w_local for _ in range(lax.axis_size('seq'))]),...]
    all_to_all x1, starting transfers between devices: 5.61 us -> 13.3 us  [per_device(): lax.all_to_all(sent, 'seq', split_axis=0, concat_axis=1, tiled=True)[0]]
  transfers between devices with their start and end apart: 27 -> 27, of which waited for: 18 -> 17; matrix products, arithmetic and copies ran while one was open for 6% -> 5% of each run, Pallas kernels for 0% -> 0%
where the time goes in v1:
time: 707 us; the launch traced here: 701 us
  waiting for transfers between devices  383 us (54%)
  local copies, waits for them, and re-layouts  104 us (15%)
  starting transfers between devices  80 us (11%)
  matrix products  77.2 us (11%)
  other arithmetic  54.9 us (8%)
    all_to_all x1, waiting for transfers between devices, per_device(): lax.all_to_all(jnp.stack([w_local for _ in range(lax.axis_size('seq'))]),...  238 us
    all_to_all x1, waiting for transfers between devices, per_device(): lax.all_to_all(back_sent, 'seq', split_axis=0, concat_axis=0, tiled=True)  48.6 us
    all_to_all x1, waiting for transfers between devices, per_device(): lax.all_to_all(sent, 'seq', split_axis=0, concat_axis=1, tiled=True)[0]  46.3 us
    ppermute x20, waiting for transfers between devices, ring_reduce_scatter(): got = lax.ppermute(buf, 'seq', perm)  35.3 us
    ppermute x20, starting transfers between devices, ring_reduce_scatter(): got = lax.ppermute(buf, 'seq', perm)  27.8 us
    convert_element_type x20, other arithmetic, ring_reduce_scatter(): (got.astype(jnp.float32) + chunk(k + 1).astype(jnp.float32)).astype(jnp.b...  22.7 us
    concatenate x1, local copies, waits for them, and re-layouts, head_pass(): jnp.concatenate([grad_keys, grad_values], axis=-1)  16.1 us
    reshape x1, local copies, waits for them, and re-layouts, head_pass(): jnp.concatenate([grad_keys, grad_values], axis=-1)  16 us
  transfers between devices with their start and end apart: 27, of which 17 were waited for; matrix products, arithmetic and copies ran while one was open for 5% of the time, Pallas kernels for 0%

profile of v1, /device:TPU:1, one launch (start us, length us, event | category | flops | bytes accessed | tf_op | source)
XLA Modules:
  0.0 701.0 jit_solution(7106950711656195648)
XLA Ops:
  1.7 5.2 stack.2
  6.9 12.3 %all-to-all-start = ((bf16[32,64,2560]{2,1,0:T(8,128)(2,1)}), bf16[32,64,2560]{2,1,0:T(8,128)(2,1)}, u32[]{:S(2)}, u32[]{:S(2)}) async-start(bf16[32,64,2560]{2,1,0:T(8,128)(2,1)} %stack.2), calls=%async_computation | async-start | bytes 20971520 | tf_op jit(solution)/shard_map/all_to_all | solution.py:104
  19.5 237.8 %all-to-all-done = bf16[32,64,2560]{2,1,0:T(8,128)(2,1)} async-done(((bf16[32,64,2560]{2,1,0:T(8,128)(2,1)}), bf16[32,64,2560]{2,1,0:T(8,128)(2,1)}, u32[]{:S(2)}, u32[]{:S(2)}) %all-to-all-start) | async-done | bytes 10485792 | tf_op jit(solution)/shard_map/all_to_all | solution.py:104
  257.3 6.9 fusion.13
  266.1 13.3 %all-to-all-start.1 = ((bf16[32,128,256]{1,2,0:T(8,128)(2,1)}), bf16[32,128,256]{1,2,0:T(8,128)(2,1)}, u32[]{:S(2)}, u32[]{:S(2)}) async-start(bf16[32,128,256]{1,2,0:T(8,128)(2,1)} %pad_maximum_fusion.1), calls=%async_computation.1 | async-start | bytes 4194304 | tf_op jit(solution)/shard_map/all_to_all | solution.py:124
  281.9 46.3 %all-to-all-done.1 = bf16[32,128,256]{1,2,0:T(8,128)(2,1)} async-done(((bf16[32,128,256]{1,2,0:T(8,128)(2,1)}), bf16[32,128,256]{1,2,0:T(8,128)(2,1)}, u32[]{:S(2)}, u32[]{:S(2)}) %all-to-all-start.1) | async-done | bytes 2097184 | tf_op jit(solution)/shard_map/all_to_all | solution.py:124
  328.2 3.3 copy.117
  331.4 2.7 fusion.73
  337.4 2.9 gather_fusion
  340.2 6.2 copy.122
  346.5 7.8 %reshape.158 = bf16[32,896,64]{1,0,2:T(8,128)(2,1)} reshape(bf16[224,128,64]{1,0,2:T(8,128)(2,1)} %copy.122) | data formatting | bytes 7340032 | tf_op jit(solution)/shard_map/reshape | solution.py:24
  354.2 3.0 gather_fusion.1
  357.2 6.2 copy.127
  363.5 7.8 %reshape.160 = bf16[32,896,64]{1,0,2:T(8,128)(2,1)} reshape(bf16[224,128,64]{1,0,2:T(8,128)(2,1)} %copy.127) | data formatting | bytes 7340032 | tf_op jit(solution)/shard_map/reshape | solution.py:25
  371.3 10.8 %fusion.77 = (f32[32,128]{1,0:T(8,128)S(1)}, f32[32,128,896]{2,1,0:T(8,128)}) fusion(pred[896]{0:T(1024)(128)(4,1)S(1)} %broadcast_bitcast_fusion, bf16[32,128,64]{2,1,0:T(8,128)(2,1)S(1)} %bitcast.153, bf16[32,896,64]{1,0,2:T(8,128)(2,1)} %reshape.158), kind=kOutput, calls=%fused_computation.119 | convolution fusion | flops 484443008 | bytes 18891648 | tf_op jit(solution)/shard_map/sub | solution.py:31
  382.1 9.3 %fusion.31 = bf16[32,128,64]{1,2,0:T(8,128)(2,1)S(1)} fusion(bf16[32,896,64]{1,0,2:T(8,128)(2,1)} %reshape.160, f32[32,128,896]{2,1,0:T(8,128)} %get-tuple-element.49, f32[32,128]{1,0:T(8,128)S(1)} %get-tuple-element.48), kind=kOutput, calls=%fused_computation.42 | convolution fusion | flops 477364224 | bytes 18890752 | tf_op jit(solution)/shard_map/gqk,gke->gqe/dot_general | solution.py:34
  391.4 9.8 %fusion.9 = f32[32,896,64]{1,2,0:T(8,128)} fusion(bf16[32,128,64]{2,1,0:T(8,128)(2,1)S(1)} %bitcast.163, f32[32,128,896]{2,1,0:T(8,128)} %get-tuple-element.49, f32[32,128]{1,0:T(8,128)S(1)} %get-tuple-element.48), kind=kOutput, calls=%fused_computation.22 | convolution fusion | flops 477102080 | bytes 22560768 | tf_op jit(solution)/shard_map/gqk,gqe->gke/dot_general | solution.py:48
  401.2 11.0 %multiply_reduce_fusion = (f32[32,128]{1,0:T(8,128)S(1)}, f32[32,128,896]{2,1,0:T(8,128)}) fusion(f32[32,128,896]{2,1,0:T(8,128)} %get-tuple-element.49, f32[32,128]{1,0:T(8,128)S(1)} %get-tuple-element.48, bf16[32,128,64]{2,1,0:T(8,128)(2,1)S(1)} %bitcast.164, bf16[32,896,64]{1,0,2:T(8,128)(2,1)S(1)} %copy-done.7), kind=kOutput, calls=%fused_computation.9 | convolution fusion | flops 480768000 | bytes 33587200 | tf_op jit(solution)/shard_map/gqe,gke->gqk/dot_general | solution.py:37
  412.2 10.9 %multiply_convert_fusion.1 = bf16[32,128,896]{2,1,0:T(8,128)(2,1)S(1)} fusion(f32[32,128,896]{2,1,0:T(8,128)} %get-tuple-element.51, f32[32,128]{1,0:T(8,128)S(1)} %get-tuple-element.50, f32[32,128,896]{2,1,0:T(8,128)} %get-tuple-element.49, f32[32,128]{1,0:T(8,128)S(1)} %get-tuple-element.48), kind=kLoop, calls=%fused_computation.8 | loop fusion | flops 14680064 | bytes 36732928 | tf_op jit(solution)/shard_map/convert_element_type | solution.py:39
  423.0 3.4 fusion.28
  426.4 4.3 broadcast_multiply_fusion
  432.3 10.5 %pad_maximum_fusion = f32[32,896,128]{1,2,0:T(8,128)} fusion(f32[32,896,64]{1,2,0:T(8,128)} %fusion.9, f32[32,896,64]{1,2,0:T(8,128)} %broadcast_multiply_fusion), kind=kLoop, calls=%fused_computation.7 | loop fusion | flops 3670016 | bytes 29360128 | tf_op jit(solution)/shard_map/concatenate | solution.py:49
  442.8 16.1 %copy.136 = f32[32,896,128]{2,1,0:T(8,128)} copy(f32[32,896,128]{1,2,0:T(8,128)} %pad_maximum_fusion) | data formatting | bytes 29360128 | tf_op jit(solution)/shard_map/concatenate | solution.py:49
  459.0 16.0 %reshape.162 = f32[224,16384]{1,0:T(8,128)} reshape(f32[32,896,128]{2,1,0:T(8,128)} %copy.136) | data formatting | bytes 29360128 | tf_op jit(solution)/shard_map/reshape | solution.py:49
  476.6 9.1 %fusion.22 = bf16[32,128,128]{2,0,1:T(8,128)(2,1)S(1)} fusion(s32[224]{0:T(256)S(1)} %eq.47, f32[224,16384]{1,0:T(8,128)} %reshape.162), kind=kOutput, calls=%fused_computation.39 | convolution fusion | flops 1409817600 | bytes 15729536 | tf_op jit(solution)/shard_map/dot_general | solution.py:56
  489.4 7.1 %all-to-all-start.2 = ((bf16[32,128,256]{2,1,0:T(8,128)(2,1)}), bf16[32,128,256]{2,1,0:T(8,128)(2,1)S(1)}, u32[]{:S(2)}, u32[]{:S(2)}) async-start(bf16[32,128,256]{2,1,0:T(8,128)(2,1)} %copy.140), calls=%async_computation.2 | async-start | bytes 4194304 | tf_op jit(solution)/shard_map/all_to_all | solution.py:142
  496.5 48.6 %all-to-all-done.2 = bf16[32,128,256]{2,1,0:T(8,128)(2,1)S(1)} async-done(((bf16[32,128,256]{2,1,0:T(8,128)(2,1)}), bf16[32,128,256]{2,1,0:T(8,128)(2,1)S(1)}, u32[]{:S(2)}, u32[]{:S(2)}) %all-to-all-start.2) | async-done | bytes 2097184 | tf_op jit(solution)/shard_map/all_to_all | solution.py:142
  549.4 4.2 multiply_convert_fusion
  553.7 2.9 dynamic-slice_bitcast_fusion
  556.6 2.7 copy-done.1
  561.7 8.6 %collective-permute-done = bf16[2048,1280]{1,0:T(8,128)(2,1)} collective-permute-done((bf16[2048,1280]{1,0:T(8,128)(2,1)}, bf16[2048,1280]{1,0:T(8,128)(2,1)}, u32[]{:S(2)}, u32[]{:S(2)}) %collective-permute-start) | collective-permute-done | bytes 5242912 | tf_op jit(solution)/shard_map/ppermute | solution.py:168
  570.3 5.4 fusion.5
  581.3 7.0 collective-permute-done.11
  594.0 4.8 collective-permute-done.12
  600.7 2.9 collective-permute-start.13
  605.4 3.4 collective-permute-done.13
  610.7 3.4 collective-permute-start.14
  620.3 3.1 collective-permute-start.15
  629.7 3.1 collective-permute-start.16
  639.0 3.1 collective-permute-start.17
  643.3 3.2 collective-permute-done.17
  656.7 3.0 collective-permute-start.20
  661.3 4.4 collective-permute-done.10
  667.1 3.3 collective-permute-done.21
  670.4 2.8 collective-permute-start.22
  673.2 2.9 collective-permute-done.22
  676.2 13.0 %collective-permute-start.23 = (bf16[64,1280]{1,0:T(8,128)(2,1)S(1)}, bf16[64,1280]{1,0:T(8,128)(2,1)S(1)}, u32[]{:S(2)}, u32[]{:S(2)}) collective-permute-start(bf16[64,1280]{1,0:T(8,128)(2,1)S(1)} %add_convert_fusion), channel_id=1, source_target_pairs={{0,32},{32,0},{64,96},{96,64},{128,160},{160,128},{192,224},{224,1... | collective-permute-start | bytes 491528 | tf_op jit(solution)/shard_map/ppermute | solution.py:180
  689.2 8.5 %fusion.21 = bf16[1,128,2048]{2,1,0:T(8,128)(2,1)} fusion(bf16[2048,2560]{1,0:T(8,128)(2,1)} %bitcast.2, bf16[128,256]{0,1:T(8,128)(2,1)S(1)} %bitcast.166, bf16[128,256]{0,1:T(8,128)(2,1)S(1)} %bitcast.168, bf16[128,2048]{0,1:T(8,128)(2,1)} %bitcast.156), kind=kOutput, calls=%fused_computation.36 | convolution fusion | flops 1344405504 | bytes 11665408 | tf_op jit(solution)/shard_map/dot_general | solution.py:155
  (118 shorter events, 74.3 us)
Async XLA Ops:
  0.6 256.7 %copy-start = (bf16[1,128,2048]{2,1,0:T(8,128)(2,1)S(1)}, bf16[1,128,2048]{2,1,0:T(8,128)(2,1)}, u32[]{:S(2)}) copy-start(bf16[1,128,2048]{2,1,0:T(8,128)(2,1)} %param.7) | copy-start | bytes 1572868
  6.9 12.3 %copy-start.10 = (bf16[1,128,2048]{2,1,0:T(8,128)(2,1)S(1)}, bf16[1,128,2048]{2,1,0:T(8,128)(2,1)}, u32[]{:S(2)}) copy-start(bf16[1,128,2048]{2,1,0:T(8,128)(2,1)} %param.13) | copy-start | bytes 1572868
  6.9 250.3 %all-to-all-start = ((bf16[32,64,2560]{2,1,0:T(8,128)(2,1)}), bf16[32,64,2560]{2,1,0:T(8,128)(2,1)}, u32[]{:S(2)}, u32[]{:S(2)}) async-start(bf16[32,64,2560]{2,1,0:T(8,128)(2,1)} %stack.2), calls=%async_computation | async-start | bytes 20971520 | tf_op jit(solution)/shard_map/all_to_all | solution.py:104
  264.2 15.2 %copy-start.11 = (s32[32]{0:T(128)S(1)}, s32[32]{0:T(128)}, u32[]{:S(2)}) copy-start(s32[32]{0:T(128)} %param.12) | copy-start | bytes 388
  266.1 62.1 %all-to-all-start.1 = ((bf16[32,128,256]{1,2,0:T(8,128)(2,1)}), bf16[32,128,256]{1,2,0:T(8,128)(2,1)}, u32[]{:S(2)}, u32[]{:S(2)}) async-start(bf16[32,128,256]{1,2,0:T(8,128)(2,1)} %pad_maximum_fusion.1), calls=%async_computation.1 | async-start | bytes 4194304 | tf_op jit(solution)/shard_map/all_to_all | solution.py:124
  363.5 7.8 %copy-start.3 = (bf16[4096,64]{1,0:T(8,128)(2,1)S(1)}, bf16[4096,64]{1,0:T(8,128)(2,1)}, u32[]{:S(2)}) copy-start(bf16[4096,64]{1,0:T(8,128)(2,1)} %get-tuple-element.39) | copy-start | bytes 1572868
  382.1 9.3 %copy-start.8 = (bf16[4096,64]{1,0:T(8,128)(2,1)S(1)}, bf16[4096,64]{1,0:T(8,128)(2,1)}, u32[]{:S(2)}) copy-start(bf16[4096,64]{1,0:T(8,128)(2,1)} %get-tuple-element.37) | copy-start | bytes 1572868
  391.4 9.8 %copy-start.7 = (bf16[32,896,64]{1,0,2:T(8,128)(2,1)S(1)}, bf16[32,896,64]{1,0,2:T(8,128)(2,1)}, u32[]{:S(2)}) copy-start(bf16[32,896,64]{1,0,2:T(8,128)(2,1)} %reshape.160) | copy-start | bytes 11010052
  412.1 10.9 %copy-start.6 = (bf16[32,896,64]{1,0,2:T(8,128)(2,1)S(1)}, bf16[32,896,64]{1,0,2:T(8,128)(2,1)}, u32[]{:S(2)}) copy-start(bf16[32,896,64]{1,0,2:T(8,128)(2,1)} %reshape.158) | copy-start | bytes 11010052
  459.0 16.1 %copy-start.9 = (bf16[32,128,64]{1,2,0:T(8,128)(2,1)S(1)}, bf16[32,128,64]{1,2,0:T(8,128)(2,1)}, u32[]{:S(2)}) copy-start(bf16[32,128,64]{1,2,0:T(8,128)(2,1)} %fusion.28) | copy-start | bytes 1572868
  489.4 55.8 %all-to-all-start.2 = ((bf16[32,128,256]{2,1,0:T(8,128)(2,1)}), bf16[32,128,256]{2,1,0:T(8,128)(2,1)S(1)}, u32[]{:S(2)}, u32[]{:S(2)}) async-start(bf16[32,128,256]{2,1,0:T(8,128)(2,1)} %copy.140), calls=%async_computation.2 | async-start | bytes 4194304 | tf_op jit(solution)/shard_map/all_to_all | solution.py:142
  548.7 5.0 copy-start.4
  553.6 5.7 copy-start.1
  559.3 11.0 %collective-permute-start = (bf16[2048,1280]{1,0:T(8,128)(2,1)}, bf16[2048,1280]{1,0:T(8,128)(2,1)}, u32[]{:S(2)}, u32[]{:S(2)}) collective-permute-start(bf16[2048,1280]{1,0:T(8,128)(2,1)} %dynamic-slice_bitcast_fusion), channel_id=1, source_target_pairs={{0,32},{32,0},{64,96},{96,64},{128,160},{160,128},{192,224},{224,1... | collective-permute-start | bytes 15728648 | tf_op jit(solution)/shard_map/ppermute | solution.py:168
  576.8 1.5 copy-start.2
  579.1 9.2 %collective-permute-start.11 = (bf16[4,64,640]{2,1,0:T(8,128)(2,1)}, bf16[4,64,640]{2,1,0:T(8,128)(2,1)}, u32[]{:S(2)}, u32[]{:S(2)}) collective-permute-start(bf16[4,64,640]{2,1,0:T(8,128)(2,1)} %dynamic-slice_bitcast_fusion.1), channel_id=1, source_target_pairs={{1,0},{2,1},{3,2},{4,3},{5,4},{6,5},{7,6},{0,7},{9,8},{10,9},{11,1... | collective-permute-start | bytes 983048 | tf_op jit(solution)/shard_map/ppermute | solution.py:83
  580.5 11.7 %collective-permute-start.1 = (bf16[4,64,640]{2,1,0:T(8,128)(2,1)}, bf16[4,64,640]{2,1,0:T(8,128)(2,1)}, u32[]{:S(2)}, u32[]{:S(2)}) collective-permute-start(bf16[4,64,640]{2,1,0:T(8,128)(2,1)} %dynamic-slice_bitcast_fusion.2), channel_id=1, source_target_pairs={{0,1},{1,2},{2,3},{3,4},{4,5},{5,6},{6,7},{7,0},{8,9},{9,10},{10,1... | collective-permute-start | bytes 983048 | tf_op jit(solution)/shard_map/ppermute | solution.py:83
  590.2 8.7 %collective-permute-start.12 = (bf16[4,64,640]{2,1,0:T(8,128)(2,1)}, bf16[4,64,640]{2,1,0:T(8,128)(2,1)}, u32[]{:S(2)}, u32[]{:S(2)}) collective-permute-start(bf16[4,64,640]{2,1,0:T(8,128)(2,1)} %fusion.46), channel_id=1, source_target_pairs={{1,0},{2,1},{3,2},{4,3},{5,4},{6,5},{7,6},{0,7},{9,8},{10,9},{11,1... | collective-permute-start | bytes 983048 | tf_op jit(solution)/shard_map/ppermute | solution.py:83
  594.0 9.6 %collective-permute-start.2 = (bf16[4,64,640]{2,1,0:T(8,128)(2,1)}, bf16[4,64,640]{2,1,0:T(8,128)(2,1)}, u32[]{:S(2)}, u32[]{:S(2)}) collective-permute-start(bf16[4,64,640]{2,1,0:T(8,128)(2,1)} %fusion.53), channel_id=1, source_target_pairs={{0,1},{1,2},{2,3},{3,4},{4,5},{5,6},{6,7},{7,0},{8,9},{9,10},{10,1... | collective-permute-start | bytes 983048 | tf_op jit(solution)/shard_map/ppermute | solution.py:83
  600.7 8.1 %collective-permute-start.13 = (bf16[4,64,640]{2,1,0:T(8,128)(2,1)}, bf16[4,64,640]{2,1,0:T(8,128)(2,1)}, u32[]{:S(2)}, u32[]{:S(2)}) collective-permute-start(bf16[4,64,640]{2,1,0:T(8,128)(2,1)} %fusion.45), channel_id=1, source_target_pairs={{1,0},{2,1},{3,2},{4,3},{5,4},{6,5},{7,6},{0,7},{9,8},{10,9},{11,1... | collective-permute-start | bytes 983048 | tf_op jit(solution)/shard_map/ppermute | solution.py:83
  605.4 8.7 %collective-permute-start.3 = (bf16[4,64,640]{2,1,0:T(8,128)(2,1)}, bf16[4,64,640]{2,1,0:T(8,128)(2,1)}, u32[]{:S(2)}, u32[]{:S(2)}) collective-permute-start(bf16[4,64,640]{2,1,0:T(8,128)(2,1)} %fusion.52), channel_id=1, source_target_pairs={{0,1},{1,2},{2,3},{3,4},{4,5},{5,6},{6,7},{7,0},{8,9},{9,10},{10,1... | collective-permute-start | bytes 983048 | tf_op jit(solution)/shard_map/ppermute | solution.py:83
  610.7 7.7 %collective-permute-start.14 = (bf16[4,64,640]{2,1,0:T(8,128)(2,1)}, bf16[4,64,640]{2,1,0:T(8,128)(2,1)}, u32[]{:S(2)}, u32[]{:S(2)}) collective-permute-start(bf16[4,64,640]{2,1,0:T(8,128)(2,1)} %fusion.44), channel_id=1, source_target_pairs={{1,0},{2,1},{3,2},{4,3},{5,4},{6,5},{7,6},{0,7},{9,8},{10,9},{11,1... | collective-permute-start | bytes 983048 | tf_op jit(solution)/shard_map/ppermute | solution.py:83
  615.9 7.5 %collective-permute-start.4 = (bf16[4,64,640]{2,1,0:T(8,128)(2,1)}, bf16[4,64,640]{2,1,0:T(8,128)(2,1)}, u32[]{:S(2)}, u32[]{:S(2)}) collective-permute-start(bf16[4,64,640]{2,1,0:T(8,128)(2,1)} %fusion.51), channel_id=1, source_target_pairs={{0,1},{1,2},{2,3},{3,4},{4,5},{5,6},{6,7},{7,0},{8,9},{9,10},{10,1... | collective-permute-start | bytes 983048 | tf_op jit(solution)/shard_map/ppermute | solution.py:83
  620.3 7.5 %collective-permute-start.15 = (bf16[4,64,640]{2,1,0:T(8,128)(2,1)}, bf16[4,64,640]{2,1,0:T(8,128)(2,1)}, u32[]{:S(2)}, u32[]{:S(2)}) collective-permute-start(bf16[4,64,640]{2,1,0:T(8,128)(2,1)} %fusion.43), channel_id=1, source_target_pairs={{1,0},{2,1},{3,2},{4,3},{5,4},{6,5},{7,6},{0,7},{9,8},{10,9},{11,1... | collective-permute-start | bytes 983048 | tf_op jit(solution)/shard_map/ppermute | solution.py:83
  625.3 7.5 %collective-permute-start.5 = (bf16[4,64,640]{2,1,0:T(8,128)(2,1)}, bf16[4,64,640]{2,1,0:T(8,128)(2,1)}, u32[]{:S(2)}, u32[]{:S(2)}) collective-permute-start(bf16[4,64,640]{2,1,0:T(8,128)(2,1)} %fusion.50), channel_id=1, source_target_pairs={{0,1},{1,2},{2,3},{3,4},{4,5},{5,6},{6,7},{7,0},{8,9},{9,10},{10,1... | collective-permute-start | bytes 983048 | tf_op jit(solution)/shard_map/ppermute | solution.py:83
  629.7 7.5 %collective-permute-start.16 = (bf16[4,64,640]{2,1,0:T(8,128)(2,1)}, bf16[4,64,640]{2,1,0:T(8,128)(2,1)}, u32[]{:S(2)}, u32[]{:S(2)}) collective-permute-start(bf16[4,64,640]{2,1,0:T(8,128)(2,1)} %fusion.42), channel_id=1, source_target_pairs={{1,0},{2,1},{3,2},{4,3},{5,4},{6,5},{7,6},{0,7},{9,8},{10,9},{11,1... | collective-permute-start | bytes 983048 | tf_op jit(solution)/shard_map/ppermute | solution.py:83
  634.6 7.5 %collective-permute-start.6 = (bf16[4,64,640]{2,1,0:T(8,128)(2,1)}, bf16[4,64,640]{2,1,0:T(8,128)(2,1)}, u32[]{:S(2)}, u32[]{:S(2)}) collective-permute-start(bf16[4,64,640]{2,1,0:T(8,128)(2,1)} %fusion.49), channel_id=1, source_target_pairs={{0,1},{1,2},{2,3},{3,4},{4,5},{5,6},{6,7},{7,0},{8,9},{9,10},{10,1... | collective-permute-start | bytes 983048 | tf_op jit(solution)/shard_map/ppermute | solution.py:83
  639.0 7.5 %collective-permute-start.17 = (bf16[4,64,640]{2,1,0:T(8,128)(2,1)}, bf16[4,64,640]{2,1,0:T(8,128)(2,1)}, u32[]{:S(2)}, u32[]{:S(2)}) collective-permute-start(bf16[4,64,640]{2,1,0:T(8,128)(2,1)} %fusion.41), channel_id=1, source_target_pairs={{1,0},{2,1},{3,2},{4,3},{5,4},{6,5},{7,6},{0,7},{9,8},{10,9},{11,1... | collective-permute-start | bytes 983048 | tf_op jit(solution)/shard_map/ppermute | solution.py:83
  643.2 8.4 %collective-permute-start.7 = (bf16[4,64,640]{2,1,0:T(8,128)(2,1)S(1)}, bf16[4,64,640]{2,1,0:T(8,128)(2,1)S(1)}, u32[]{:S(2)}, u32[]{:S(2)}) collective-permute-start(bf16[4,64,640]{2,1,0:T(8,128)(2,1)S(1)} %fusion.48), channel_id=1, source_target_pairs={{0,1},{1,2},{2,3},{3,4},{4,5},{5,6},{6,7},{7,0},{8,9},{9,10},{10,1... | collective-permute-start | bytes 983048 | tf_op jit(solution)/shard_map/ppermute | solution.py:83
  647.6 5.1 collective-permute-start.18
  651.7 4.9 collective-permute-start.8
  652.7 3.9 collective-permute-start.19
  656.6 4.6 collective-permute-start.9
  656.7 4.6 collective-permute-start.20
  661.2 4.6 collective-permute-start.10
  665.8 4.6 collective-permute-start.21
  670.4 5.8 collective-permute-start.22
  676.2 21.5 %copy-start.5 = (bf16[32,128,64]{2,1,0:T(8,128)(2,1)S(1)}, bf16[32,128,64]{2,1,0:T(8,128)(2,1)}, u32[]{:S(2)}) copy-start(bf16[32,128,64]{2,1,0:T(8,128)(2,1)} %get-tuple-element.35) | copy-start | bytes 1572868
  676.2 22.9 %collective-permute-start.23 = (bf16[64,1280]{1,0:T(8,128)(2,1)S(1)}, bf16[64,1280]{1,0:T(8,128)(2,1)S(1)}, u32[]{:S(2)}, u32[]{:S(2)}) collective-permute-start(bf16[64,1280]{1,0:T(8,128)(2,1)S(1)} %add_convert_fusion), channel_id=1, source_target_pairs={{0,32},{32,0},{64,96},{96,64},{128,160},{160,128},{192,224},{224,1... | collective-permute-start | bytes 491528 | tf_op jit(solution)/shard_map/ppermute | solution.py:180
